TPU v7x, 256 devices: a whole 4x4x8 slice. The times are simulated.
256 devices in a mesh: seq: 64 (over z, y, x_lo), head: 4 (over x_hi, core).
Axes of the slice: x: 4 (x_hi: 2, x_lo: 2; x = x_hi * 2 + x_lo), y: 4, z: 8, core: 2. Of those that a mesh axis runs over, the one named last changes fastest.
Arguments:
- features: bfloat16 [8192, 960], P('seq', 'head'), may hold values from -36 to 36
- conv_weight: bfloat16 [960, 120, 128], P('head'), may hold values from -0.046875 to 0.046875
- ln_gain: float32 [960], replicated, may hold values from 0.5 to 1.5
- ln_bias: float32 [960], replicated, may hold values from -4 to 4
- query_weight: bfloat16 [8, 115200], P('head'), may hold values from -0.875 to 0.875
- key_weight: bfloat16 [8, 115200], P('head'), may hold values from -0.875 to 0.875
- value_weight: bfloat16 [8, 115200], P('head'), may hold values from -0.1875 to 0.1875
- out_weight: bfloat16 [960, 960], P('head'), may hold values from -0.1875 to 0.1875
- proj_weight: bfloat16 [960, 1024], P(None, 'head'), may hold values from -0.10085894 to 0.10085894
- targets: bfloat16 [8192, 1024], P('seq', 'head'), may hold values from -3.125 to 3.125
- mask_positions: int32 [1024], P('seq'), may hold values from 0 to 8191, as said below
- distractors: int32 [1024, 100], P('seq'), may hold values from 0 to 8191, as said below
- loss_weight: float32 [1024], P('seq'), may hold values from 0.2 to 2
Outputs:
- encoded: bfloat16 [8192, 960], P('seq', 'head')
- proj_grad: float32 [960, 1024], P(None, 'head')
- target_grad: float32 [8192, 1024], P('seq', 'head')
Inputs may be any that keep to these rules, and one draw needn't show every extreme that they name: `mask_positions`: the entries of aligned block d of 16 are distinct frames of d * 128 to (d + 1) * 128 - 1. `distractors`: call value // 128 the block of an entry. In every aligned block of 16 rows exactly 50 entries name one block, the same block for all row blocks and drawn from the seed; the remaining 16 * 100 - 50 entries of the row block are spread over the other blocks as evenly as possible.
All inputs are finite; a program needn't handle non-finite values.
Results may differ from a plain program's by a relative error of at most 0.007.
Values may be sent and summed in bfloat16 or wider, within the bound.
No kernel may reach another device: no remote copies, remote signals or barrier semaphores. Data moves between devices by JAX's collectives and lax.ppermute only.
A program may use at most 128 MiB of HBM per device.

v0:
```python
import math
import jax
import jax.numpy as jnp
from jax import lax
from jax.sharding import PartitionSpec as P

TAPS = 128
NORM_EPS = 1e-05
EPSILON = 1e-06
SOFTMAX_WARMTH = 0.1


def with_halo(shard, sides, width):
    for axis, dim in sides:
        size, length = (lax.axis_size(axis), shard.shape[dim])
        up = [(i, (i + 1) % size) for i in range(size - 1)]
        down = [(j, i) for i, j in up]
        last = lax.slice_in_dim(shard, length - width, length, axis=dim)
        first = lax.slice_in_dim(shard, 0, width, axis=dim)
        before = lax.ppermute(last, axis, up)
        after = lax.ppermute(first, axis, down)
        shard = jnp.concatenate([before, shard, after], axis=dim)
    return shard


def layer_norm(hidden, gain_terms, bias_terms):
    wide = hidden.astype(jnp.float32)
    center = jnp.mean(wide, axis=-1, keepdims=True)
    spread = jnp.mean((wide - center) ** 2, axis=-1, keepdims=True)
    return ((wide - center) * lax.rsqrt(spread + NORM_EPS) * gain_terms + bias_terms).astype(
        jnp.bfloat16
    )


def head_project(normed, flat_weight, head_count, head_dim):
    full_width = normed.shape[1]
    head_weight = flat_weight.reshape(head_count, full_width, head_dim)
    result = jnp.einsum("tw,hwd->thd", normed, head_weight, preferred_element_type=jnp.float32)
    return result.astype(jnp.bfloat16)


def contrast_terms(products, target_sq, context_sq, weight_matrix):
    inv_context = lax.rsqrt(context_sq + EPSILON)
    inv_target = lax.rsqrt(target_sq + EPSILON)
    cosine_scores = products * inv_context[:, None] * inv_target
    exponentiated = jnp.exp(cosine_scores / SOFTMAX_WARMTH)
    softmax_shares = exponentiated / jnp.sum(exponentiated, axis=1, keepdims=True)
    leading_term = (lax.broadcasted_iota(jnp.int32, softmax_shares.shape, 1) == 0).astype(
        jnp.float32
    )
    logit_slope = weight_matrix[:, None] * (softmax_shares - leading_term) / SOFTMAX_WARMTH
    along = logit_slope * inv_context[:, None] * inv_target
    shrink = logit_slope * cosine_scores * inv_target * inv_target
    spread = jnp.sum(logit_slope * cosine_scores, axis=1) * inv_context * inv_context
    return (along, shrink, spread)


def attend_block(running, key_block, value_block, query_heads, head_count, score_scale):
    numer, denom, highest = running
    row_count = key_block.shape[0]
    key_heads = key_block.reshape(row_count, head_count, -1)
    value_heads = value_block.reshape(row_count, head_count, -1)
    scores = (
        jnp.einsum("qhd,khd->hqk", query_heads, key_heads, preferred_element_type=jnp.float32)
        * score_scale
    )
    new_high = jnp.maximum(highest, jnp.max(scores, axis=2))
    factor = jnp.exp(highest - new_high)
    weights = jnp.exp(scores - new_high[:, :, None])
    denom = denom * factor + jnp.sum(weights, axis=2)
    numer = numer * factor[:, :, None] + jnp.einsum(
        "hqk,khd->hqd",
        weights.astype(jnp.bfloat16),
        value_heads,
        preferred_element_type=jnp.float32,
    )
    return (numer, denom, new_high)


def take_rows(asked, targets):
    return targets[jnp.maximum(asked, 0)]


def place_rows(asked_flat, rows_flat, frame_count):
    segment_ids = jnp.where(asked_flat >= 0, asked_flat, frame_count)
    return jax.ops.segment_sum(rows_flat, segment_ids, num_segments=frame_count + 1)[:frame_count]


def per_device(
    features,
    conv_weight,
    ln_gain,
    ln_bias,
    query_weight,
    key_weight,
    value_weight,
    out_weight,
    proj_weight,
    targets,
    mask_positions,
    distractors,
    loss_weight,
):
    frame_count, local_width = features.shape
    head_dim = conv_weight.shape[1]
    head_count = local_width // head_dim
    extended = with_halo(features, (("seq", 0),), TAPS // 2)
    position = lax.conv_general_dilated(
        extended[None],
        conv_weight,
        (1,),
        "VALID",
        dimension_numbers=("NWC", "OIW", "NWC"),
        feature_group_count=head_count,
        preferred_element_type=jnp.float32,
    )[0, :frame_count]
    hidden = (features.astype(jnp.float32) + jax.nn.gelu(position, approximate=False)).astype(
        jnp.bfloat16
    )
    normed = layer_norm(lax.all_gather(hidden, "head", axis=1, tiled=True), ln_gain, ln_bias)
    query_heads = head_project(normed, query_weight, head_count, head_dim)
    key_here = head_project(normed, key_weight, head_count, head_dim).reshape(
        frame_count, local_width
    )
    value_here = head_project(normed, value_weight, head_count, head_dim).reshape(
        frame_count, local_width
    )
    score_scale = 1.0 / math.sqrt(head_dim)
    initial = (
        jnp.zeros((head_count, frame_count, head_dim), jnp.float32),
        jnp.zeros((head_count, frame_count), jnp.float32),
        jnp.full((head_count, frame_count), -1e30, jnp.float32),
    )
    running = initial
    key_piece = lax.all_gather(key_here, "seq", axis=0, tiled=True)
    value_piece = lax.all_gather(value_here, "seq", axis=0, tiled=True)
    row_count = key_piece.shape[0]

    def advance(partial_value, blocks):
        return (
            attend_block(partial_value, blocks[0], blocks[1], query_heads, head_count, score_scale),
            None,
        )

    running, _ = lax.scan(
        advance,
        running,
        (
            key_piece.reshape(row_count // 512, 512, -1),
            value_piece.reshape(row_count // 512, 512, -1),
        ),
    )
    numer, denom, _ = running
    attended = (
        (numer / denom[:, :, None])
        .astype(jnp.bfloat16)
        .transpose(1, 0, 2)
        .reshape(frame_count, local_width)
    )
    branch = lax.psum_scatter(
        jnp.dot(attended, out_weight, preferred_element_type=jnp.float32).astype(jnp.bfloat16),
        "head",
        scatter_dimension=1,
        tiled=True,
    ).astype(jnp.float32)
    encoded = (hidden.astype(jnp.float32) + branch).astype(jnp.bfloat16)
    seq_index = lax.axis_index("seq")
    seq_count = lax.axis_size("seq")
    local_mask = mask_positions - seq_index * frame_count
    masked_full = lax.all_gather(encoded[local_mask], "head", axis=1, tiled=True)
    context = jnp.dot(masked_full, proj_weight, preferred_element_type=jnp.float32)
    masked_count, distract_count = distractors.shape
    request_count = masked_count * distract_count
    capacity = 2 * request_count // seq_count
    target_width = targets.shape[1]
    flat_dist = distractors.reshape(-1)
    owners = flat_dist // frame_count
    row_ids = flat_dist % frame_count
    owner_hits = (owners[:, None] == jnp.arange(seq_count, dtype=jnp.int32)[None, :]).astype(
        jnp.int32
    )
    earlier = jnp.cumsum(owner_hits, axis=0) - owner_hits
    slot_ids = jnp.sum(earlier * owner_hits, axis=1)
    buckets = owners * capacity + slot_ids
    requests = (
        jnp.full((seq_count * capacity,), -1, jnp.int32)
        .at[buckets]
        .set(row_ids)
        .reshape(seq_count, capacity)
    )
    positive = targets[local_mask]
    asked = lax.all_to_all(requests, "seq", split_axis=0, concat_axis=0, tiled=True)
    found = take_rows(asked, targets)
    returned = lax.all_to_all(found, "seq", split_axis=0, concat_axis=0, tiled=True)
    fetched = returned.reshape(seq_count * capacity, target_width)[buckets].reshape(
        masked_count, distract_count, target_width
    )
    cands = jnp.concatenate([positive[:, None, :], fetched], axis=1).astype(jnp.float32)
    products_here = jnp.einsum("me,mke->mk", context, cands, precision=lax.Precision.HIGHEST)
    target_sq_here = jnp.sum(cands * cands, axis=2)
    context_sq_here = jnp.sum(context * context, axis=1)
    products, target_sq, context_sq = lax.psum(
        (products_here, target_sq_here, context_sq_here), "head"
    )
    along, shrink, spread = contrast_terms(products, target_sq, context_sq, loss_weight)
    cand_grads = along[:, :, None] * context[:, None, :] - shrink[:, :, None] * cands
    context_grad = (
        jnp.einsum("mk,mke->me", along, cands, precision=lax.Precision.HIGHEST)
        - spread[:, None] * context
    )
    target_grad = (
        jnp.zeros((frame_count, target_width), jnp.float32).at[local_mask].add(cand_grads[:, 0])
    )
    outgoing = (
        jnp.zeros((seq_count * capacity, target_width), jnp.float32)
        .at[buckets]
        .set(cand_grads[:, 1:].reshape(request_count, target_width))
    )
    incoming = (
        lax.all_to_all(
            outgoing.reshape(seq_count, capacity, target_width).astype(jnp.bfloat16),
            "seq",
            split_axis=0,
            concat_axis=0,
            tiled=True,
        )
        .astype(jnp.float32)
        .reshape(seq_count * capacity, target_width)
    )
    target_grad = target_grad + place_rows(asked.reshape(-1), incoming, frame_count)
    proj_term = jnp.einsum(
        "mw,me->we", masked_full.astype(jnp.float32), context_grad, precision=lax.Precision.HIGHEST
    )
    proj_grad = lax.psum(proj_term, "seq")
    return (encoded, proj_grad, target_grad)


def solution(mesh):
    return jax.shard_map(
        per_device,
        mesh=mesh,
        in_specs=(
            P("seq", "head"),
            P("head", None, None),
            P(),
            P(),
            P("head", None),
            P("head", None),
            P("head", None),
            P("head", None),
            P(None, "head"),
            P("seq", "head"),
            P("seq"),
            P("seq", None),
            P("seq"),
        ),
        out_specs=(P("seq", "head"), P(None, "head"), P("seq", "head")),
        check_vma=False,
    )
```

profile of v0, /device:TPU:8, one launch (start us, length us, event | category | flops | bytes accessed | tf_op | source)
XLA Modules:
  0.0 1307.5 jit_solution(7271690625776360250)
XLA Ops:
  8.2 3.4 collective-permute-start
  11.6 3.3 collective-permute-start.1
  15.0 10.7 copy.41
  27.6 17.3 %fusion.67 = f32[1,129,2,120]{3,0,2,1:T(1,128)S(1)} fusion(bf16[1,256,2,120]{3,0,2,1:T(2,128)(2,1)S(1)} %copy.40, bf16[2,120,120,128]{2,1,0,3:T(8,128)(2,1)} %copy.41), kind=kOutput, calls=%fused_computation.135 | convolution fusion | flops 951091200 | bytes 7619520 | tf_op jit(solution)/shard_map/conv_general_dilated | solution.py:108
  45.3 7.2 all_gather.12
  57.4 18.1 %reduce-window.6 = s32[64,13,128]{2,1,0:T(8,128)S(1)} reduce-window(s32[64,13,128]{2,1,0:T(8,128)S(1)} %reshape.259, s32[]{:T(128)} %constant.57.clone.1), window={size=1x1x128 pad=0_0x0_0x127_0}, to_apply=%region_7.8 | reduce-window | flops 13524992 | bytes 851972 | tf_op jit(solution)/shard_map/reduce-window
  76.7 8.8 scatter_custom_fusion
  86.3 12.8 all-to-all-start
  100.6 7.8 all-to-all-done
  110.0 9.9 gather_fusion.2
  119.9 1.5 reshape.279
  121.4 6.3 all-to-all-start.1
  128.5 194.0 %all-gather.7.cloned.1.call-done = bf16[8192,240]{0,1:T(8,128)(2,1)} async-done(((bf16[128,240]{0,1:T(8,128)(2,1)}), bf16[8192,240]{0,1:T(8,128)(2,1)}) %all-gather.7.cloned.1.call-update) | async-done | bytes 3932176 | tf_op jit(solution)/shard_map/all_gather | solution.py:136
  322.5 4.4 copy.77
  326.9 243.4 %all-gather.5.cloned.1.call-done = bf16[8192,240]{0,1:T(8,128)(2,1)} async-done(((bf16[128,240]{0,1:T(8,128)(2,1)}), bf16[8192,240]{0,1:T(8,128)(2,1)}) %all-gather.5.cloned.1.call-update) | async-done | bytes 3932176 | tf_op jit(solution)/shard_map/all_gather | solution.py:135
  570.3 4.4 copy.78
  574.8 29.4 %while.15 = (s32[]{:T(128)}, f32[2,128,120]{1,2,0:T(8,128)S(1)}, f32[2,128]{1,0:T(2,128)S(1)}, f32[2,128]{1,0:T(2,128)S(1)}, bf16[16,512,240]{1,2,0:T(8,128)(2,1...) while((s32[]{:T(128)}, f32[2,128,120]{1,2,0:T(8,128)S(1)}, ...), condition=%wide.region_5.6_spmd.clone, body=%wide.region_2.5_spmd.clone.sunk | while | flops 63794432 | bytes 3371117 | solution.py:145
  606.0 2.5 reshape.253
  608.5 5.6 gather_fusion.3
  614.7 20.9 %reduce-scatter.2.cloned.1.call-done = bf16[128,240]{0,1:T(8,128)(2,1)} async-done(((bf16[128,960]{0,1:T(8,128)(2,1)}), bf16[128,240]{0,1:T(8,128)(2,1)}) %reduce-scatter.2.cloned.1.call-update) | async-done | bytes 61456 | tf_op jit(solution)/shard_map/reduce_scatter | solution.py:160
  637.1 6.7 all-gather.1
  645.1 13.6 %all-reduce.1 = (f32[16,101]{1,0:T(8,128)S(1)}, f32[16]{0:T(128)S(1)}, f32[16,101]{1,0:T(8,128)S(1)}) all-reduce(f32[16,101]{1,0:T(8,128)S(1)} %fusion.7, f32[16]{0:T(128)S(1)} %get-tuple-element.115, f32[16,101]{1,0:T(8,128)S(1)} %bitcast.173), channel_id=1, replica_groups=mesh['seq'=64,'head'=4] {'head'}, use_global_device_ids=true, to_apply=%region_15.16 | all-reduce | flops 3248 | bytes 25984 | tf_op jit(solution)/shard_map/psum | solution.py:202
  662.4 12.8 scatter_custom_fusion.1
  675.2 2.1 convert_element_type.73
  677.3 1.5 convert_element_type.74
  678.8 11.5 all-to-all-start.2
  691.2 1.6 fusion.43
  693.8 40.9 %all-to-all-done.2 = bf16[64,50,256]{2,1,0:T(8,128)(2,1)S(1)} async-done(((bf16[64,50,256]{2,1,0:T(8,128)(2,1)}), bf16[64,50,256]{2,1,0:T(8,128)(2,1)S(1)}, u32[]{:S(2)}, u32[]{:S(2)}) %all-to-all-start.2) | async-done | bytes 1638432 | tf_op jit(solution)/shard_map/all_to_all | solution.py:220
  734.8 1.9 reshape.314
  736.7 20.7 %scatter_custom_fusion.2 = f32[129,256]{1,0:T(8,128)S(1)} fusion(s32[3200]{0:T(1024)S(1)} %fusion.48, f32[3200,256]{1,0:T(8,128)} %reshape.314, f32[]{:T(128)} %constant.68.clone.1), kind=kCustom, calls=%fused_computation.78 | custom fusion | flops 819200 | bytes 132608 | tf_op jit(solution)/shard_map/scatter-add | solution.py:86
  758.1 540.6 %all-reduce.4.cloned.1.call-done = f32[960,256]{1,0:T(8,128)} async-done(((f32[960,256]{1,0:T(8,128)}), f32[960,256]{1,0:T(8,128)}) %all-reduce.4.cloned.1.call-update) | async-done | bytes 983056 | tf_op jit(solution)/shard_map/psum | solution.py:234
  1298.8 2.2 copy.94
  (226 shorter events, 53.9 us)
Async XLA Ops:
  7.2 597.1 %copy-start = (bf16[240,960]{1,0:T(8,128)(2,1)S(1)}, bf16[240,960]{1,0:T(8,128)(2,1)}, u32[]{:S(2)}) copy-start(bf16[240,960]{1,0:T(8,128)(2,1)} %param.22) | copy-start | bytes 1382404
  7.2 315.4 %all-gather.7.cloned.1.call-start = ((), (), s32[]{:S(2)}) async-start(), calls=%async_computation.5 | async-start | bytes 3993600 | tf_op jit(solution)/shard_map/all_gather | solution.py:136
  8.2 19.0 %collective-permute-start = (bf16[64,240]{0,1:T(8,128)(2,1)S(1)}, bf16[64,240]{0,1:T(8,128)(2,1)S(1)}, u32[]{:S(2)}, u32[]{:S(2)}) collective-permute-start(bf16[64,240]{0,1:T(8,128)(2,1)S(1)} %get-tuple-element.106), channel_id=1, source_target_pairs={{0,4},{4,8},{8,12},{12,16},{16,20},{20,24},{24,28},{28,32},{32,36}... | collective-permute-start | bytes 92168 | tf_op jit(solution)/shard_map/ppermute | solution.py:20
  11.6 15.6 %collective-permute-start.1 = (bf16[64,240]{0,1:T(8,128)(2,1)S(1)}, bf16[64,240]{0,1:T(8,128)(2,1)S(1)}, u32[]{:S(2)}, u32[]{:S(2)}) collective-permute-start(bf16[64,240]{0,1:T(8,128)(2,1)S(1)} %get-tuple-element.107), channel_id=1, source_target_pairs={{4,0},{8,4},{12,8},{16,12},{20,16},{24,20},{28,24},{32,28},{36,32}... | collective-permute-start | bytes 92168 | tf_op jit(solution)/shard_map/ppermute | solution.py:21
  15.0 10.8 copy-start.5
  25.7 1.5 copy-start.3
  27.6 25.3 %copy-start.12 = (f32[960]{0:T(1024)S(1)}, f32[960]{0:T(1024)}, u32[]{:S(2)}) copy-start(f32[960]{0:T(1024)} %param.18) | copy-start | bytes 11524
  27.6 25.3 %copy-start.13 = (f32[960]{0:T(1024)S(1)}, f32[960]{0:T(1024)}, u32[]{:S(2)}) copy-start(f32[960]{0:T(1024)} %param.17) | copy-start | bytes 11524
  44.9 9.4 copy-start.6
  54.1 3.0 copy-start.10
  54.1 516.2 %all-gather.5.cloned.1.call-start = ((), (), s32[]{:S(2)}) async-start(), calls=%async_computation.4 | async-start | bytes 3993600 | tf_op jit(solution)/shard_map/all_gather | solution.py:135
  75.8 23.3 %copy-start.7 = (bf16[2,115200]{1,0:T(2,128)(2,1)S(1)}, bf16[2,115200]{1,0:T(2,128)(2,1)}, u32[]{:S(2)}) copy-start(bf16[2,115200]{1,0:T(2,128)(2,1)} %param.19) | copy-start | bytes 1382404
  76.4 33.5 %copy-start.1 = (bf16[128,256]{1,0:T(8,128)(2,1)S(1)}, bf16[128,256]{1,0:T(8,128)(2,1)}, u32[]{:S(2)}) copy-start(bf16[128,256]{1,0:T(8,128)(2,1)} %param.24) | copy-start | bytes 196612
  86.3 22.2 %all-to-all-start = ((s32[64,1,50]{2,1,0:T(1,128)}), s32[64,1,50]{2,1,0:T(1,128)S(1)}, u32[]{:S(2)}, u32[]{:S(2)}) async-start(s32[64,1,50]{2,1,0:T(1,128)} %bitcast.24), calls=%async_computation.1 | async-start | bytes 65536 | tf_op jit(solution)/shard_map/all_to_all | solution.py:192
  121.4 484.6 %all-to-all-start.1 = ((bf16[64,50,256]{2,1,0:T(8,128)(2,1)}), bf16[64,50,256]{2,1,0:T(8,128)(2,1)}, u32[]{:S(2)}, u32[]{:S(2)}) async-start(bf16[64,50,256]{2,1,0:T(8,128)(2,1)} %reshape.279), calls=%async_computation.2 | async-start | bytes 3670016 | tf_op jit(solution)/shard_map/all_to_all | solution.py:194
  127.7 507.9 %reduce-scatter.2.cloned.1.call-start = ((), (), s32[]{:S(2)}) async-start(), calls=%async_computation.6 | async-start | bytes 307200 | tf_op jit(solution)/shard_map/reduce_scatter | solution.py:160
  574.8 30.6 %copy-start.14 = (s32[16]{0:T(128)S(1)}, s32[16]{0:T(128)}, u32[]{:S(2)}) copy-start(s32[16]{0:T(128)} %param.25) | copy-start | bytes 196
  614.1 29.9 %copy-start.4 = (bf16[960,256]{1,0:T(8,128)(2,1)S(1)}, bf16[960,256]{1,0:T(8,128)(2,1)}, u32[]{:S(2)}) copy-start(bf16[960,256]{1,0:T(8,128)(2,1)} %param.23) | copy-start | bytes 1474564
  614.3 44.5 %copy-start.11 = (f32[16]{0:T(128)S(1)}, f32[16]{0:T(128)}, u32[]{:S(2)}) copy-start(f32[16]{0:T(128)} %param.27) | copy-start | bytes 196
  636.4 23.3 %copy-start.8 = (bf16[128,240]{0,1:T(8,128)(2,1)}, bf16[128,240]{0,1:T(8,128)(2,1)S(1)}, u32[]{:S(2)}) copy-start(bf16[128,240]{0,1:T(8,128)(2,1)S(1)} %add_convert_fusion) | copy-start | bytes 184324
  659.7 1.2 copy-start.2
  678.8 56.0 %all-to-all-start.2 = ((bf16[64,50,256]{2,1,0:T(8,128)(2,1)}), bf16[64,50,256]{2,1,0:T(8,128)(2,1)S(1)}, u32[]{:S(2)}, u32[]{:S(2)}) async-start(bf16[64,50,256]{2,1,0:T(8,128)(2,1)} %convert_element_type.74), calls=%async_computation.3 | async-start | bytes 3670016 | tf_op jit(solution)/shard_map/all_to_all | solution.py:220
  690.2 608.5 %all-reduce.4.cloned.1.call-start = ((), (), s32[]{:S(2)}) async-start(), calls=%async_computation.7 | async-start | bytes 1966080 | tf_op jit(solution)/shard_map/psum | solution.py:234
  758.1 542.8 %copy-start.9 = (f32[128,256]{1,0:T(8,128)}, f32[128,256]{1,0:T(8,128)S(1)}, u32[]{:S(2)}) copy-start(f32[128,256]{1,0:T(8,128)S(1)} %scatter_custom_fusion.3) | copy-start | bytes 393220
Sparse Core Ops, SparseCore 0:
  54.2 268.2 all-gather.6
  324.8 245.4 all-gather.4
  605.4 30.1 reduce-scatter.1
  694.2 604.5 all-reduce.3
where the time goes:
time: 1310 us
  waiting for transfers between devices  1050 us (80%)
  local copies, waits for them, and re-layouts  97.4 us (7%)
  other arithmetic  49.3 us (4%)
  starting transfers between devices  38.1 us (3%)
  matrix products  32.3 us (2%)
  blocking collectives  27.5 us (2%)
  between operations  14.4 us (1%)
    psum x1, waiting for transfers between devices, per_device(): proj_grad = lax.psum(proj_term, 'seq')  541 us
    all_gather x1, waiting for transfers between devices, per_device(): key_piece = lax.all_gather(key_here, 'seq', axis=0, tiled=True)  243 us
    all_gather x1, waiting for transfers between devices, per_device(): value_piece = lax.all_gather(value_here, 'seq', axis=0, tiled=True)  194 us
    all_to_all x1, waiting for transfers between devices, per_device(): lax.all_to_all(outgoing.reshape(seq_count, capacity, target_width).astype...  40.9 us
  transfers between devices with their start and end apart: 9, of which 6 were waited for; matrix products, arithmetic and copies ran while one was open for 10% of the time, Pallas kernels for 0%

commit v1 on v0

--- a/solution.py
+++ b/solution.py
@@ -231,7 +231,7 @@
     proj_term = jnp.einsum(
         "mw,me->we", masked_full.astype(jnp.float32), context_grad, precision=lax.Precision.HIGHEST
     )
-    proj_grad = lax.psum(proj_term, "seq")
+    proj_grad = jnp.sum(lax.all_gather(proj_term, "seq"), axis=0)
     return (encoded, proj_grad, target_grad)
 
 

time: 1310 us -> 2060 us (1.57)
  waiting for transfers between devices: 1050 us -> 1770 us
    all_gather x0 -> x1, waiting for transfers between devices: none -> 1250 us  [per_device(): proj_grad = jnp.sum(lax.all_gather(proj_term, 'seq'), axis=0)]
    psum x1 -> x0, waiting for transfers between devices: 541 us -> none  [per_device(): proj_grad = lax.psum(proj_term, 'seq')]
  transfers between devices with their start and end apart: 9 -> 9, of which waited for: 6 -> 6; matrix products, arithmetic and copies ran while one was open for 10% -> 7% of each run, Pallas kernels for 0% -> 0%
where the time goes in v1:
time: 2060 us; the launch traced here: 2050 us
  waiting for transfers between devices  1770 us (86%)
  local copies, waits for them, and re-layouts  96.2 us (5%)
  other arithmetic  69.8 us (3%)
  starting transfers between devices  38 us (2%)
  matrix products  32.3 us (2%)
  blocking collectives  27.5 us (1%)
    all_gather x1, waiting for transfers between devices, per_device(): proj_grad = jnp.sum(lax.all_gather(proj_term, 'seq'), axis=0)  1250 us
    all_gather x1, waiting for transfers between devices, per_device(): key_piece = lax.all_gather(key_here, 'seq', axis=0, tiled=True)  245 us
    all_gather x1, waiting for transfers between devices, per_device(): value_piece = lax.all_gather(value_here, 'seq', axis=0, tiled=True)  192 us
    all_to_all x1, waiting for transfers between devices, per_device(): lax.all_to_all(outgoing.reshape(seq_count, capacity, target_width).astype...  54.9 us
  transfers between devices with their start and end apart: 9, of which 6 were waited for; matrix products, arithmetic and copies ran while one was open for 7% of the time, Pallas kernels for 0%

profile of v1, /device:TPU:8, one launch (start us, length us, event | category | flops | bytes accessed | tf_op | source)
XLA Modules:
  0.0 2053.6 jit_solution(4974644809966801104)
XLA Ops:
  8.2 3.4 collective-permute-start
  11.6 3.3 collective-permute-start.1
  15.0 10.7 copy.41
  27.6 17.3 fusion.67
  45.3 7.2 all_gather.18
  57.4 18.1 reduce-window.6
  76.7 8.8 scatter_custom_fusion
  86.3 12.8 all-to-all-start
  101.4 7.1 all-to-all-done
  110.0 9.9 gather_fusion.2
  120.0 1.5 reshape.279
  121.4 6.5 all-to-all-start.1
  128.5 192.1 %all-gather.9.cloned.1.call-done = bf16[8192,240]{0,1:T(8,128)(2,1)} async-done(((bf16[128,240]{0,1:T(8,128)(2,1)}), bf16[8192,240]{0,1:T(8,128)(2,1)}) %all-gather.9.cloned.1.call-update) | async-done | bytes 3932176 | tf_op jit(solution)/shard_map/all_gather | solution.py:136
  320.7 4.4 copy.77
  325.1 245.5 %all-gather.7.cloned.1.call-done = bf16[8192,240]{0,1:T(8,128)(2,1)} async-done(((bf16[128,240]{0,1:T(8,128)(2,1)}), bf16[8192,240]{0,1:T(8,128)(2,1)}) %all-gather.7.cloned.1.call-update) | async-done | bytes 3932176 | tf_op jit(solution)/shard_map/all_gather | solution.py:135
  570.5 4.5 copy.78
  575.1 29.4 %while.15 = (s32[]{:T(128)}, f32[2,128,120]{1,2,0:T(8,128)S(1)}, f32[2,128]{1,0:T(2,128)S(1)}, f32[2,128]{1,0:T(2,128)S(1)}, bf16[16,512,240]{1,2,0:T(8,128)(2,1...) while((s32[]{:T(128)}, f32[2,128,120]{1,2,0:T(8,128)S(1)}, ...), condition=%wide.region_5.6_spmd.clone, body=%wide.region_2.5_spmd.clone.sunk | while | flops 63794432 | bytes 3371117 | solution.py:145
  606.6 2.5 reshape.253
  609.1 5.6 gather_fusion.3
  615.3 20.6 %reduce-scatter.2.cloned.1.call-done = bf16[128,240]{0,1:T(8,128)(2,1)} async-done(((bf16[128,960]{0,1:T(8,128)(2,1)}), bf16[128,240]{0,1:T(8,128)(2,1)}) %reduce-scatter.2.cloned.1.call-update) | async-done | bytes 61456 | tf_op jit(solution)/shard_map/reduce_scatter | solution.py:160
  637.4 6.7 all-gather.2
  645.4 13.6 all-reduce.1
  659.9 1.6 fusion.43
  664.9 12.8 scatter_custom_fusion.1
  677.7 2.1 convert_element_type.73
  679.8 1.5 convert_element_type.74
  681.3 11.5 all-to-all-start.2
  693.9 54.9 %all-to-all-done.2 = bf16[64,50,256]{2,1,0:T(8,128)(2,1)S(1)} async-done(((bf16[64,50,256]{2,1,0:T(8,128)(2,1)}), bf16[64,50,256]{2,1,0:T(8,128)(2,1)S(1)}, u32[]{:S(2)}, u32[]{:S(2)}) %all-to-all-start.2) | async-done | bytes 1638432 | tf_op jit(solution)/shard_map/all_to_all | solution.py:220
  748.8 1.9 reshape.314
  750.7 20.7 %scatter_custom_fusion.2 = f32[129,256]{1,0:T(8,128)S(1)} fusion(s32[3200]{0:T(1024)S(1)} %fusion.48, f32[3200,256]{1,0:T(8,128)} %reshape.314, f32[]{:T(128)} %constant.68.clone.1), kind=kCustom, calls=%fused_computation.78 | custom fusion | flops 819200 | bytes 132608 | tf_op jit(solution)/shard_map/scatter-add | solution.py:86
  772.2 1254.3 %all-gather.11.cloned.1.call-done = f32[61440,256]{1,0:T(8,128)} async-done(((f32[960,256]{1,0:T(8,128)}), f32[61440,256]{1,0:T(8,128)}) %all-gather.11.cloned.1.call-update) | async-done | bytes 62914576 | tf_op jit(solution)/shard_map/all_gather | solution.py:234
  2026.5 20.6 %reduce_sum.91 = f32[960,256]{1,0:T(8,128)} reduce(f32[64,960,256]{2,1,0:T(8,128)} %bitcast.148, f32[]{:T(128)} %constant.68.clone.1), dimensions={0}, to_apply=%region_18.19 | reduce | flops 15482880 | bytes 63897604 | tf_op jit(solution)/shard_map/reduce_sum | solution.py:234
  (230 shorter events, 54.5 us)
Async XLA Ops:
  7.2 597.4 %copy-start = (bf16[240,960]{1,0:T(8,128)(2,1)S(1)}, bf16[240,960]{1,0:T(8,128)(2,1)}, u32[]{:S(2)}) copy-start(bf16[240,960]{1,0:T(8,128)(2,1)} %param.22) | copy-start | bytes 1382404
  7.2 313.5 %all-gather.9.cloned.1.call-start = ((), (), s32[]{:S(2)}) async-start(), calls=%async_computation.5 | async-start | bytes 3993600 | tf_op jit(solution)/shard_map/all_gather | solution.py:136
  8.2 19.0 collective-permute-start
  11.6 15.6 collective-permute-start.1
  15.0 10.8 copy-start.7
  25.7 1.5 copy-start.4
  27.6 25.3 %copy-start.14 = (f32[960]{0:T(1024)S(1)}, f32[960]{0:T(1024)}, u32[]{:S(2)}) copy-start(f32[960]{0:T(1024)} %param.18) | copy-start | bytes 11524
  27.6 25.3 %copy-start.15 = (f32[960]{0:T(1024)S(1)}, f32[960]{0:T(1024)}, u32[]{:S(2)}) copy-start(f32[960]{0:T(1024)} %param.17) | copy-start | bytes 11524
  44.9 9.4 copy-start.8
  54.1 3.0 copy-start.12
  54.1 516.5 %all-gather.7.cloned.1.call-start = ((), (), s32[]{:S(2)}) async-start(), calls=%async_computation.4 | async-start | bytes 3993600 | tf_op jit(solution)/shard_map/all_gather | solution.py:135
  75.8 23.3 %copy-start.9 = (bf16[2,115200]{1,0:T(2,128)(2,1)S(1)}, bf16[2,115200]{1,0:T(2,128)(2,1)}, u32[]{:S(2)}) copy-start(bf16[2,115200]{1,0:T(2,128)(2,1)} %param.19) | copy-start | bytes 1382404
  76.4 33.6 %copy-start.2 = (bf16[128,256]{1,0:T(8,128)(2,1)S(1)}, bf16[128,256]{1,0:T(8,128)(2,1)}, u32[]{:S(2)}) copy-start(bf16[128,256]{1,0:T(8,128)(2,1)} %param.24) | copy-start | bytes 196612
  86.3 22.2 %all-to-all-start = ((s32[64,1,50]{2,1,0:T(1,128)}), s32[64,1,50]{2,1,0:T(1,128)S(1)}, u32[]{:S(2)}, u32[]{:S(2)}) async-start(s32[64,1,50]{2,1,0:T(1,128)} %bitcast.24), calls=%async_computation.1 | async-start | bytes 65536 | tf_op jit(solution)/shard_map/all_to_all | solution.py:192
  121.4 6.5 copy-start.6
  121.4 485.1 %all-to-all-start.1 = ((bf16[64,50,256]{2,1,0:T(8,128)(2,1)}), bf16[64,50,256]{2,1,0:T(8,128)(2,1)}, u32[]{:S(2)}, u32[]{:S(2)}) async-start(bf16[64,50,256]{2,1,0:T(8,128)(2,1)} %reshape.279), calls=%async_computation.2 | async-start | bytes 3670016 | tf_op jit(solution)/shard_map/all_to_all | solution.py:194
  127.9 508.0 %reduce-scatter.2.cloned.1.call-start = ((), (), s32[]{:S(2)}) async-start(), calls=%async_computation.6 | async-start | bytes 307200 | tf_op jit(solution)/shard_map/reduce_scatter | solution.py:160
  575.1 30.8 %copy-start.16 = (s32[16]{0:T(128)S(1)}, s32[16]{0:T(128)}, u32[]{:S(2)}) copy-start(s32[16]{0:T(128)} %param.25) | copy-start | bytes 196
  605.6 1420.8 %all-gather.11.cloned.1.call-start = ((), (), s32[]{:S(2)}) async-start(), calls=%async_computation.7 | async-start | bytes 63897600 | tf_op jit(solution)/shard_map/all_gather | solution.py:234
  614.7 29.6 %copy-start.5 = (bf16[960,256]{1,0:T(8,128)(2,1)S(1)}, bf16[960,256]{1,0:T(8,128)(2,1)}, u32[]{:S(2)}) copy-start(bf16[960,256]{1,0:T(8,128)(2,1)} %param.23) | copy-start | bytes 1474564
  614.8 44.3 %copy-start.13 = (f32[16]{0:T(128)S(1)}, f32[16]{0:T(128)}, u32[]{:S(2)}) copy-start(f32[16]{0:T(128)} %param.27) | copy-start | bytes 196
  636.7 23.2 %copy-start.10 = (bf16[128,240]{0,1:T(8,128)(2,1)}, bf16[128,240]{0,1:T(8,128)(2,1)S(1)}, u32[]{:S(2)}) copy-start(bf16[128,240]{0,1:T(8,128)(2,1)S(1)} %add_convert_fusion) | copy-start | bytes 184324
  662.2 1.2 copy-start.3
  681.3 67.5 %all-to-all-start.2 = ((bf16[64,50,256]{2,1,0:T(8,128)(2,1)}), bf16[64,50,256]{2,1,0:T(8,128)(2,1)S(1)}, u32[]{:S(2)}, u32[]{:S(2)}) async-start(bf16[64,50,256]{2,1,0:T(8,128)(2,1)} %convert_element_type.74), calls=%async_computation.3 | async-start | bytes 3670016 | tf_op jit(solution)/shard_map/all_to_all | solution.py:220
  772.1 1274.9 %copy-start.11 = (f32[128,256]{1,0:T(8,128)}, f32[128,256]{1,0:T(8,128)S(1)}, u32[]{:S(2)}) copy-start(f32[128,256]{1,0:T(8,128)S(1)} %scatter_custom_fusion.3) | copy-start | bytes 393220
  2026.5 20.6 %copy-start.1 = (bf16[240,960]{1,0:T(8,128)(2,1)S(1)}, bf16[240,960]{1,0:T(8,128)(2,1)}, u32[]{:S(2)}) copy-start(bf16[240,960]{1,0:T(8,128)(2,1)} %param.22) | copy-start | bytes 1382404
Sparse Core Ops, SparseCore 0:
  54.2 266.3 all-gather.8
  322.9 247.5 all-gather.6
  605.7 30.1 reduce-scatter.1
  661.6 1364.7 all-gather.10
